TPU v7x, 128 devices: a whole 4x4x4 slice. The times are simulated.
128 devices in a mesh: segment: 4 (over x), fsdp: 16 (over y, z_hi, core), rep: 2 (over z_lo).
Axes of the slice: x: 4, y: 4, z: 4 (z_hi: 2, z_lo: 2; z = z_hi * 2 + z_lo), core: 2. Of those that a mesh axis runs over, the one named last changes fastest.
Arguments:
- token_ids: int32 [128, 128], P('fsdp'), may hold values from 0 to 127
- seq_lengths: int32 [128], P('fsdp'), may hold values from 32 to 128, as said below
- quant_scores: int32 [128], P('fsdp'), may hold values from 0 to 64
- embed_table: bfloat16 [128, 4096], replicated, may hold values from -6 to 6
- prior_weight: bfloat16 [4, 4096, 4096], P('segment', None, 'rep'), may hold values from -0.09375 to 0.09375
- prior_gain: float32 [4, 4096], P('segment'), may hold values from 0.25 to 1.75
- final_gain: float32 [4096], replicated, may hold values from 0.25 to 1.75
- head_weight: bfloat16 [4096, 128], replicated, may hold values from -0.25 to 0.25
- agent_down: bfloat16 [4096, 256], P('fsdp'), may hold values from -0.09375 to 0.09375
- agent_up: bfloat16 [4096, 256], P('fsdp'), may hold values from -0.375 to 0.375
Outputs:
- down_gradient: float32 [4096, 256], P(('segment', 'fsdp', 'rep'))
- up_gradient: float32 [4096, 256], P(('segment', 'fsdp', 'rep'))
Inputs may be any that keep to these rules, and one draw needn't show every extreme that they name: `seq_lengths`: every sequence keeps at least 32 tokens, and some sequence in every draw has all 128.
All inputs are finite; a program needn't handle non-finite values.
Results may differ from a plain program's by a relative error of at most 0.0081.
Values may be sent and summed in bfloat16 or wider, within the bound.
No kernel may reach another device: no remote copies, remote signals or barrier semaphores. Data moves between devices by JAX's collectives and lax.ppermute only.
A program may use at most 128 MiB of HBM per device.

v0:
```python
import jax
import jax.numpy as jnp
from jax import lax
from jax.sharding import PartitionSpec as P

LEVELS = 64
epsilon = 1e-05
sigma_weight = 2.0


def passed_along(x, axis, by):
    size = lax.axis_size(axis)
    pairs = [(i, i + by) for i in range(size) if 0 <= i + by < size]
    return lax.ppermute(x, axis, pairs)


def spread(x, axis, root):
    mine = lax.axis_index(axis) == root
    return lax.psum(jnp.where(mine, x, jnp.zeros_like(x)), axis)


def rms_scale(values):
    squares = jnp.mean(values * values, axis=-1, keepdims=True)
    return lax.rsqrt(squares + epsilon)


def lookup_rows(row_ids, embed_table):
    vocab_size = embed_table.shape[0]
    column = jnp.arange(vocab_size, dtype=jnp.int32)
    onehot = (row_ids[:, None] == column[None, :]).astype(jnp.bfloat16)
    return jnp.dot(onehot, embed_table, preferred_element_type=jnp.float32).astype(jnp.bfloat16)


def picked_logprob(logprob, targets):
    vocab_size = logprob.shape[-1]
    column = jnp.arange(vocab_size, dtype=jnp.int32)
    return jnp.sum(jnp.where(column[None, :] == targets[:, None], logprob, 0.0), axis=-1)


def on_device(
    token_ids,
    seq_lengths,
    quant_scores,
    embed_table,
    prior_weight,
    prior_gain,
    final_gain,
    head_weight,
    agent_down,
    agent_up,
):
    segments = lax.axis_size("segment")
    replicas = lax.axis_size("rep")
    segment_pos = lax.axis_index("segment")
    rep_pos = lax.axis_index("rep")
    group_seqs, seq_len = token_ids.shape
    model_width = embed_table.shape[1]
    vocab_size = embed_table.shape[0]
    half_width = prior_weight.shape[2]
    per_device = group_seqs // (segments * replicas)
    micro_count = 4
    total_rows = group_seqs * seq_len
    block_rows = total_rows // micro_count
    tick_count = micro_count + segments - 1
    flat_ids = token_ids.reshape(-1)
    weight_local = prior_weight[0]
    gain_local = prior_gain[0]
    is_first = segment_pos == 0
    is_last = segment_pos == segments - 1

    def apply_segment(current):
        wide_rows = current.astype(jnp.float32)
        normed = (wide_rows * rms_scale(wide_rows) * gain_local).astype(jnp.bfloat16)
        update = jnp.dot(normed, weight_local, preferred_element_type=jnp.float32)
        own_half = lax.dynamic_slice_in_dim(wide_rows, rep_pos * half_width, half_width, 1)
        return (own_half + update).astype(jnp.bfloat16)

    def skip_segment(current):
        return jnp.zeros((block_rows, half_width), jnp.bfloat16)

    def segment_step(tick_pos, received_full):
        micro_pos = tick_pos - segment_pos
        active = (micro_pos >= 0) & (micro_pos < micro_count)
        fresh_pos = jnp.clip(tick_pos, 0, micro_count - 1)
        embedded = lookup_rows(
            lax.dynamic_slice_in_dim(flat_ids, fresh_pos * block_rows, block_rows, 0), embed_table
        )
        current = jnp.where(is_first, embedded, received_full)
        result = lax.cond(active, apply_segment, skip_segment, current)
        return (active, jnp.clip(micro_pos, 0, micro_count - 1), result)

    def store_block(stored, active, slot_pos, block):
        previous = lax.dynamic_slice_in_dim(stored, slot_pos * block_rows, block_rows, 0)
        chosen = jnp.where(active & is_last, block, previous)
        return lax.dynamic_update_slice_in_dim(stored, chosen, slot_pos * block_rows, 0)

    def tick_whole(tick_pos, state_pair):
        incoming, stored = state_pair
        active, slot_pos, result = segment_step(tick_pos, incoming)
        joined = lax.all_gather(result, "rep", axis=1, tiled=True)
        stored = store_block(stored, active, slot_pos, joined)
        incoming = passed_along(joined, "segment", 1)
        return (incoming, stored)

    initial = (
        jnp.zeros((block_rows, model_width), jnp.bfloat16),
        jnp.zeros((total_rows, model_width), jnp.bfloat16),
    )
    final_rows = lax.fori_loop(0, tick_count, tick_whole, initial)[1]
    positions = jnp.arange(seq_len, dtype=jnp.int32)
    next_ids = jnp.concatenate([token_ids[:, 1:], token_ids[:, :1]], axis=1)
    live_mask = (positions[None, :] < seq_lengths[:, None] - 1).astype(jnp.float32)
    counts = (seq_lengths - 1).astype(jnp.float32)

    def prior_scores(rows_bf):
        wide_rows = rows_bf.astype(jnp.float32)
        prior_final = (wide_rows * rms_scale(wide_rows) * final_gain).astype(jnp.bfloat16)
        logprob = jax.nn.log_softmax(
            jnp.dot(prior_final, head_weight, preferred_element_type=jnp.float32), axis=-1
        )
        token_terms = picked_logprob(logprob, next_ids.reshape(-1)).reshape(group_seqs, seq_len)
        return jnp.sum(token_terms * live_mask, axis=1) / counts

    def no_scores(rows_bf):
        return jnp.zeros((group_seqs,), jnp.float32)

    prior_group = lax.cond(is_last, prior_scores, no_scores, final_rows)
    prior_group = spread(prior_group, "segment", segments - 1)
    own_seq = (segment_pos * replicas + rep_pos) * per_device
    prior_mine = lax.dynamic_slice_in_dim(prior_group, own_seq, per_device, 0)
    mine_ids = lax.dynamic_slice_in_dim(token_ids, own_seq, per_device, 0).reshape(-1)
    mine_next = lax.dynamic_slice_in_dim(next_ids, own_seq, per_device, 0).reshape(-1)
    mine_live = lax.dynamic_slice_in_dim(live_mask, own_seq, per_device, 0)
    mine_counts = lax.dynamic_slice_in_dim(counts, own_seq, per_device, 0)
    mine_scores = lax.dynamic_slice_in_dim(quant_scores, own_seq, per_device, 0)
    down_full, up_full = (
        lax.all_gather(agent_down, "fsdp", axis=0, tiled=True),
        lax.all_gather(agent_up, "fsdp", axis=0, tiled=True),
    )
    start_wide = lookup_rows(mine_ids, embed_table).astype(jnp.float32)
    unit_rows = (start_wide * rms_scale(start_wide)).astype(jnp.bfloat16)
    latent = jnp.dot(unit_rows, down_full, preferred_element_type=jnp.float32).astype(jnp.bfloat16)
    hidden = start_wide + lax.dot_general(
        latent, up_full, (((1,), (1,)), ((), ())), preferred_element_type=jnp.float32
    )
    inverse = rms_scale(hidden)
    agent_final = (hidden * inverse * final_gain).astype(jnp.bfloat16)
    logprob = jax.nn.log_softmax(
        jnp.dot(agent_final, head_weight, preferred_element_type=jnp.float32), axis=-1
    )
    agent_ll = (
        jnp.sum(picked_logprob(logprob, mine_next).reshape(per_device, seq_len) * mine_live, axis=1)
        / mine_counts
    )
    margin = prior_mine + sigma_weight * mine_scores.astype(jnp.float32) / LEVELS - agent_ll
    row_factor = ((2.0 * margin / mine_counts)[:, None] * mine_live).reshape(-1)
    column = jnp.arange(vocab_size, dtype=jnp.int32)
    onehot_next = (mine_next[:, None] == column[None, :]).astype(jnp.float32)
    logit_grad = (row_factor[:, None] * (jnp.exp(logprob) - onehot_next)).astype(jnp.bfloat16)
    scaled_grad = (
        lax.dot_general(
            logit_grad, head_weight, (((1,), (1,)), ((), ())), preferred_element_type=jnp.float32
        )
        * final_gain
    )
    hidden_grad = (
        inverse * scaled_grad
        - hidden
        * inverse
        * inverse
        * inverse
        * jnp.mean(hidden * scaled_grad, axis=-1, keepdims=True)
    ).astype(jnp.bfloat16)
    up_grad = lax.dot_general(
        hidden_grad, latent, (((0,), (0,)), ((), ())), preferred_element_type=jnp.float32
    )
    latent_grad = jnp.dot(hidden_grad, up_full, preferred_element_type=jnp.float32).astype(
        jnp.bfloat16
    )
    down_grad = lax.dot_general(
        unit_rows, latent_grad, (((0,), (0,)), ((), ())), preferred_element_type=jnp.float32
    )
    down_share, up_share = (
        lax.psum_scatter(down_grad, ("segment", "fsdp", "rep"), scatter_dimension=0, tiled=True),
        lax.psum_scatter(up_grad, ("segment", "fsdp", "rep"), scatter_dimension=0, tiled=True),
    )
    return (down_share, up_share)


def solution(mesh):
    placed = (
        P("fsdp", None),
        P("fsdp"),
        P("fsdp"),
        P(),
        P("segment", None, "rep"),
        P("segment", None),
        P(),
        P(),
        P("fsdp", None),
        P("fsdp", None),
    )
    return jax.shard_map(
        on_device,
        mesh=mesh,
        in_specs=placed,
        out_specs=(P(("segment", "fsdp", "rep"), None), P(("segment", "fsdp", "rep"), None)),
        check_vma=False,
    )
```

profile of v0, /device:TPU:0, one launch (start us, length us, event | category | flops | bytes accessed | tf_op | source)
XLA Modules:
  0.0 2145.9 jit_solution(12127194747232947936)
XLA Ops:
  8.3 4.3 broadcast_in_dim.30
  12.6 715.6 %while.15 = (s32[]{:T(128)}, bf16[256,4096]{1,0:T(8,128)(2,1)S(1)}, bf16[1024,4096]{1,0:T(8,128)(2,1)}, s32[]{:T(128)}, s32[1024]{0:T(1024)S(1)}, /*index=5*/bf1...) while((s32[]{:T(128)}, bf16[256,4096]{1,0:T(8,128)(2,1)S(1)}, ...), condition=%wide.region_6.7_spmd, body=%wide.region_2.6_spmd.sunk | while | flops 4573921792 | bytes 63987248 | solution.py:109
  12.7 0.7 convolution_convert_fusion.5
  13.5 14.8 conditional.4
  13.5 2.6 multiply_reduce_fusion
  16.2 12.1 fusion
  28.3 1.0 copy-done
  29.3 35.9 %all-gather.8.cloned.1.call-done = bf16[256,4096]{1,0:T(8,128)(2,1)} async-done(((bf16[256,2048]{1,0:T(8,128)(2,1)}), bf16[256,4096]{1,0:T(8,128)(2,1)}) %all-gather.8.cloned.1.call-update) | async-done | bytes 2097168 | tf_op jit(solution)/shard_map/while/body/eval_jaxpr/all_gather | solution.py:100
  65.2 3.5 collective-permute-start
  68.7 3.8 select_dynamic-update-slice_fusion.2
  72.4 41.1 %collective-permute-done = bf16[256,4096]{1,0:T(8,128)(2,1)S(1)} collective-permute-done((bf16[256,4096]{1,0:T(8,128)(2,1)}, bf16[256,4096]{1,0:T(8,128)(2,1)S(1)}, u32[]{:S(2)}, u32[]{:S(2)}) %collective-permute-start) | collective-permute-done | bytes 2097184 | tf_op jit(solution)/shard_map/while/body/eval_jaxpr/ppermute | solution.py:14
  113.6 0.7 convolution_convert_fusion.5
  114.4 14.8 conditional.4
  114.4 2.6 multiply_reduce_fusion
  117.0 12.1 fusion
  129.2 1.0 copy-done
  130.2 36.2 %all-gather.8.cloned.1.call-done = bf16[256,4096]{1,0:T(8,128)(2,1)} async-done(((bf16[256,2048]{1,0:T(8,128)(2,1)}), bf16[256,4096]{1,0:T(8,128)(2,1)}) %all-gather.8.cloned.1.call-update) | async-done | bytes 2097168 | tf_op jit(solution)/shard_map/while/body/eval_jaxpr/all_gather | solution.py:100
  166.4 3.5 collective-permute-start
  169.9 3.7 select_dynamic-update-slice_fusion.2
  173.6 41.2 %collective-permute-done = bf16[256,4096]{1,0:T(8,128)(2,1)S(1)} collective-permute-done((bf16[256,4096]{1,0:T(8,128)(2,1)}, bf16[256,4096]{1,0:T(8,128)(2,1)S(1)}, u32[]{:S(2)}, u32[]{:S(2)}) %collective-permute-start) | collective-permute-done | bytes 2097184 | tf_op jit(solution)/shard_map/while/body/eval_jaxpr/ppermute | solution.py:14
  214.8 0.7 convolution_convert_fusion.5
  215.6 14.8 conditional.4
  215.6 2.6 multiply_reduce_fusion
  218.3 12.1 fusion
  230.4 1.0 copy-done
  231.4 37.7 %all-gather.8.cloned.1.call-done = bf16[256,4096]{1,0:T(8,128)(2,1)} async-done(((bf16[256,2048]{1,0:T(8,128)(2,1)}), bf16[256,4096]{1,0:T(8,128)(2,1)}) %all-gather.8.cloned.1.call-update) | async-done | bytes 2097168 | tf_op jit(solution)/shard_map/while/body/eval_jaxpr/all_gather | solution.py:100
  269.1 3.5 collective-permute-start
  272.6 3.7 select_dynamic-update-slice_fusion.2
  276.4 41.1 %collective-permute-done = bf16[256,4096]{1,0:T(8,128)(2,1)S(1)} collective-permute-done((bf16[256,4096]{1,0:T(8,128)(2,1)}, bf16[256,4096]{1,0:T(8,128)(2,1)S(1)}, u32[]{:S(2)}, u32[]{:S(2)}) %collective-permute-start) | collective-permute-done | bytes 2097184 | tf_op jit(solution)/shard_map/while/body/eval_jaxpr/ppermute | solution.py:14
  317.6 0.7 convolution_convert_fusion.5
  318.3 14.8 conditional.4
  318.3 2.6 multiply_reduce_fusion
  321.0 12.1 fusion
  333.1 1.0 copy-done
  334.1 37.7 %all-gather.8.cloned.1.call-done = bf16[256,4096]{1,0:T(8,128)(2,1)} async-done(((bf16[256,2048]{1,0:T(8,128)(2,1)}), bf16[256,4096]{1,0:T(8,128)(2,1)}) %all-gather.8.cloned.1.call-update) | async-done | bytes 2097168 | tf_op jit(solution)/shard_map/while/body/eval_jaxpr/all_gather | solution.py:100
  371.8 3.5 collective-permute-start
  375.4 3.7 select_dynamic-update-slice_fusion.2
  379.1 41.1 %collective-permute-done = bf16[256,4096]{1,0:T(8,128)(2,1)S(1)} collective-permute-done((bf16[256,4096]{1,0:T(8,128)(2,1)}, bf16[256,4096]{1,0:T(8,128)(2,1)S(1)}, u32[]{:S(2)}, u32[]{:S(2)}) %collective-permute-start) | collective-permute-done | bytes 2097184 | tf_op jit(solution)/shard_map/while/body/eval_jaxpr/ppermute | solution.py:14
  420.3 0.7 convolution_convert_fusion.5
  421.2 1.0 copy-done
  422.2 52.4 %all-gather.8.cloned.1.call-done = bf16[256,4096]{1,0:T(8,128)(2,1)} async-done(((bf16[256,2048]{1,0:T(8,128)(2,1)}), bf16[256,4096]{1,0:T(8,128)(2,1)}) %all-gather.8.cloned.1.call-update) | async-done | bytes 2097168 | tf_op jit(solution)/shard_map/while/body/eval_jaxpr/all_gather | solution.py:100
  474.6 3.5 collective-permute-start
  478.1 3.7 select_dynamic-update-slice_fusion.2
  481.8 41.1 %collective-permute-done = bf16[256,4096]{1,0:T(8,128)(2,1)S(1)} collective-permute-done((bf16[256,4096]{1,0:T(8,128)(2,1)}, bf16[256,4096]{1,0:T(8,128)(2,1)S(1)}, u32[]{:S(2)}, u32[]{:S(2)}) %collective-permute-start) | collective-permute-done | bytes 2097184 | tf_op jit(solution)/shard_map/while/body/eval_jaxpr/ppermute | solution.py:14
  523.0 0.7 convolution_convert_fusion.5
  523.9 1.0 copy-done
  524.9 52.4 %all-gather.8.cloned.1.call-done = bf16[256,4096]{1,0:T(8,128)(2,1)} async-done(((bf16[256,2048]{1,0:T(8,128)(2,1)}), bf16[256,4096]{1,0:T(8,128)(2,1)}) %all-gather.8.cloned.1.call-update) | async-done | bytes 2097168 | tf_op jit(solution)/shard_map/while/body/eval_jaxpr/all_gather | solution.py:100
  577.3 3.5 collective-permute-start
  580.8 3.7 select_dynamic-update-slice_fusion.2
  584.6 41.1 %collective-permute-done = bf16[256,4096]{1,0:T(8,128)(2,1)S(1)} collective-permute-done((bf16[256,4096]{1,0:T(8,128)(2,1)}, bf16[256,4096]{1,0:T(8,128)(2,1)S(1)}, u32[]{:S(2)}, u32[]{:S(2)}) %collective-permute-start) | collective-permute-done | bytes 2097184 | tf_op jit(solution)/shard_map/while/body/eval_jaxpr/ppermute | solution.py:14
  626.7 1.0 copy-done
  627.7 52.1 %all-gather.8.cloned.1.call-done = bf16[256,4096]{1,0:T(8,128)(2,1)} async-done(((bf16[256,2048]{1,0:T(8,128)(2,1)}), bf16[256,4096]{1,0:T(8,128)(2,1)}) %all-gather.8.cloned.1.call-update) | async-done | bytes 2097168 | tf_op jit(solution)/shard_map/while/body/eval_jaxpr/all_gather | solution.py:100
  679.7 3.5 collective-permute-start
  683.3 3.7 select_dynamic-update-slice_fusion.2
  687.0 41.1 %collective-permute-done = bf16[256,4096]{1,0:T(8,128)(2,1)S(1)} collective-permute-done((bf16[256,4096]{1,0:T(8,128)(2,1)}, bf16[256,4096]{1,0:T(8,128)(2,1)S(1)}, u32[]{:S(2)}, u32[]{:S(2)}) %collective-permute-start) | collective-permute-done | bytes 2097184 | tf_op jit(solution)/shard_map/while/body/eval_jaxpr/ppermute | solution.py:14
  729.6 21.7 %psum.7 = f32[8]{0:T(128)S(1)} all-reduce(f32[8]{0:T(128)S(1)} %broadcast_select_fusion), channel_id=1, replica_groups=mesh['segment'=4,'fsdp'=16,'rep'=2] {'segment'}, use_global_device_ids=true, to_apply=%region_14.15 | all-reduce | flops 8 | bytes 64 | tf_op jit(solution)/shard_map/psum | solution.py:19
  755.1 26.0 %all-gather.4.cloned.1.call-done = bf16[4096,256]{1,0:T(8,128)(2,1)} async-done(((bf16[256,256]{1,0:T(8,128)(2,1)}), bf16[4096,256]{1,0:T(8,128)(2,1)}) %all-gather.4.cloned.1.call-update) | async-done | bytes 2097168 | tf_op jit(solution)/shard_map/all_gather | solution.py:137
  781.1 2.1 convolution_convert_fusion.3
  783.2 47.1 %all-gather.6.cloned.1.call-done = bf16[4096,256]{1,0:T(8,128)(2,1)} async-done(((bf16[256,256]{1,0:T(8,128)(2,1)}), bf16[4096,256]{1,0:T(8,128)(2,1)}) %all-gather.6.cloned.1.call-update) | async-done | bytes 2097168 | tf_op jit(solution)/shard_map/all_gather | solution.py:138
  830.2 2.5 multiply_reduce_fusion.2
  837.4 5.2 fusion.13
  842.6 2.7 fusion.29
  845.4 646.0 %reduce-scatter.3.cloned.1.call-done = f32[32,256]{1,0:T(8,128)} async-done(((f32[4096,256]{1,0:T(8,128)}), f32[32,256]{1,0:T(8,128)}) %reduce-scatter.3.cloned.1.call-update) | async-done | bytes 32784 | tf_op jit(solution)/shard_map/reduce_scatter | solution.py:184
  1491.3 647.0 %reduce-scatter.5.cloned.1.call-done = f32[32,256]{1,0:T(8,128)} async-done(((f32[4096,256]{1,0:T(8,128)}), f32[32,256]{1,0:T(8,128)}) %reduce-scatter.5.cloned.1.call-update) | async-done | bytes 32784 | tf_op jit(solution)/shard_map/reduce_scatter | solution.py:185
  (85 shorter events, 8.9 us)
Async XLA Ops:
  8.2 4.3 copy-start.2
  8.3 4.3 copy-start.5
  8.3 4.3 copy-start.6
  12.6 716.9 %copy-start.7 = (s32[8]{0:T(128)S(1)}, s32[8]{0:T(128)}, u32[]{:S(2)}) copy-start(s32[8]{0:T(128)} %param.17) | copy-start | bytes 100
  12.6 717.0 %copy-start.4 = (f32[4096]{0:T(1024)S(1)}, f32[4096]{0:T(1024)}, u32[]{:S(2)}) copy-start(f32[4096]{0:T(1024)} %param.22) | copy-start | bytes 49156
  12.6 52.6 %all-gather.8.cloned.1.call-start = ((), (), s32[]{:S(2)}) async-start(), calls=%async_computation.6 | async-start | bytes 3145728 | tf_op jit(solution)/shard_map/while/body/eval_jaxpr/all_gather | solution.py:100
  28.3 1.0 copy-start
  65.2 48.4 %collective-permute-start = (bf16[256,4096]{1,0:T(8,128)(2,1)}, bf16[256,4096]{1,0:T(8,128)(2,1)S(1)}, u32[]{:S(2)}, u32[]{:S(2)}) collective-permute-start(bf16[256,4096]{1,0:T(8,128)(2,1)} %all-gather.8.cloned.1.call-done), channel_id=1, source_target_pairs={{0,32},{32,64},{64,96},{1,33},{33,65},{65,97},{2,34},{34,66},{66,9... | collective-permute-start | bytes 6291464 | tf_op jit(solution)/shard_map/while/body/eval_jaxpr/ppermute | solution.py:14
  113.5 52.8 %all-gather.8.cloned.1.call-start = ((), (), s32[]{:S(2)}) async-start(), calls=%async_computation.6 | async-start | bytes 3145728 | tf_op jit(solution)/shard_map/while/body/eval_jaxpr/all_gather | solution.py:100
  129.2 1.0 copy-start
  166.4 48.4 %collective-permute-start = (bf16[256,4096]{1,0:T(8,128)(2,1)}, bf16[256,4096]{1,0:T(8,128)(2,1)S(1)}, u32[]{:S(2)}, u32[]{:S(2)}) collective-permute-start(bf16[256,4096]{1,0:T(8,128)(2,1)} %all-gather.8.cloned.1.call-done), channel_id=1, source_target_pairs={{0,32},{32,64},{64,96},{1,33},{33,65},{65,97},{2,34},{34,66},{66,9... | collective-permute-start | bytes 6291464 | tf_op jit(solution)/shard_map/while/body/eval_jaxpr/ppermute | solution.py:14
  214.8 54.3 %all-gather.8.cloned.1.call-start = ((), (), s32[]{:S(2)}) async-start(), calls=%async_computation.6 | async-start | bytes 3145728 | tf_op jit(solution)/shard_map/while/body/eval_jaxpr/all_gather | solution.py:100
  230.4 1.0 copy-start
  269.1 48.4 %collective-permute-start = (bf16[256,4096]{1,0:T(8,128)(2,1)}, bf16[256,4096]{1,0:T(8,128)(2,1)S(1)}, u32[]{:S(2)}, u32[]{:S(2)}) collective-permute-start(bf16[256,4096]{1,0:T(8,128)(2,1)} %all-gather.8.cloned.1.call-done), channel_id=1, source_target_pairs={{0,32},{32,64},{64,96},{1,33},{33,65},{65,97},{2,34},{34,66},{66,9... | collective-permute-start | bytes 6291464 | tf_op jit(solution)/shard_map/while/body/eval_jaxpr/ppermute | solution.py:14
  317.5 54.3 %all-gather.8.cloned.1.call-start = ((), (), s32[]{:S(2)}) async-start(), calls=%async_computation.6 | async-start | bytes 3145728 | tf_op jit(solution)/shard_map/while/body/eval_jaxpr/all_gather | solution.py:100
  333.1 1.0 copy-start
  371.8 48.4 %collective-permute-start = (bf16[256,4096]{1,0:T(8,128)(2,1)}, bf16[256,4096]{1,0:T(8,128)(2,1)S(1)}, u32[]{:S(2)}, u32[]{:S(2)}) collective-permute-start(bf16[256,4096]{1,0:T(8,128)(2,1)} %all-gather.8.cloned.1.call-done), channel_id=1, source_target_pairs={{0,32},{32,64},{64,96},{1,33},{33,65},{65,97},{2,34},{34,66},{66,9... | collective-permute-start | bytes 6291464 | tf_op jit(solution)/shard_map/while/body/eval_jaxpr/ppermute | solution.py:14
  420.2 54.3 %all-gather.8.cloned.1.call-start = ((), (), s32[]{:S(2)}) async-start(), calls=%async_computation.6 | async-start | bytes 3145728 | tf_op jit(solution)/shard_map/while/body/eval_jaxpr/all_gather | solution.py:100
  421.2 1.0 copy-start
  474.6 48.4 %collective-permute-start = (bf16[256,4096]{1,0:T(8,128)(2,1)}, bf16[256,4096]{1,0:T(8,128)(2,1)S(1)}, u32[]{:S(2)}, u32[]{:S(2)}) collective-permute-start(bf16[256,4096]{1,0:T(8,128)(2,1)} %all-gather.8.cloned.1.call-done), channel_id=1, source_target_pairs={{0,32},{32,64},{64,96},{1,33},{33,65},{65,97},{2,34},{34,66},{66,9... | collective-permute-start | bytes 6291464 | tf_op jit(solution)/shard_map/while/body/eval_jaxpr/ppermute | solution.py:14
  523.0 54.3 %all-gather.8.cloned.1.call-start = ((), (), s32[]{:S(2)}) async-start(), calls=%async_computation.6 | async-start | bytes 3145728 | tf_op jit(solution)/shard_map/while/body/eval_jaxpr/all_gather | solution.py:100
  523.9 1.0 copy-start
  577.3 48.4 %collective-permute-start = (bf16[256,4096]{1,0:T(8,128)(2,1)}, bf16[256,4096]{1,0:T(8,128)(2,1)S(1)}, u32[]{:S(2)}, u32[]{:S(2)}) collective-permute-start(bf16[256,4096]{1,0:T(8,128)(2,1)} %all-gather.8.cloned.1.call-done), channel_id=1, source_target_pairs={{0,32},{32,64},{64,96},{1,33},{33,65},{65,97},{2,34},{34,66},{66,9... | collective-permute-start | bytes 6291464 | tf_op jit(solution)/shard_map/while/body/eval_jaxpr/ppermute | solution.py:14
  625.7 54.1 %all-gather.8.cloned.1.call-start = ((), (), s32[]{:S(2)}) async-start(), calls=%async_computation.6 | async-start | bytes 3145728 | tf_op jit(solution)/shard_map/while/body/eval_jaxpr/all_gather | solution.py:100
  626.7 1.0 copy-start
  679.7 48.4 %collective-permute-start = (bf16[256,4096]{1,0:T(8,128)(2,1)}, bf16[256,4096]{1,0:T(8,128)(2,1)S(1)}, u32[]{:S(2)}, u32[]{:S(2)}) collective-permute-start(bf16[256,4096]{1,0:T(8,128)(2,1)} %all-gather.8.cloned.1.call-done), channel_id=1, source_target_pairs={{0,32},{32,64},{64,96},{1,33},{33,65},{65,97},{2,34},{34,66},{66,9... | collective-permute-start | bytes 6291464 | tf_op jit(solution)/shard_map/while/body/eval_jaxpr/ppermute | solution.py:14
  728.1 52.9 %all-gather.4.cloned.1.call-start = ((), (), s32[]{:S(2)}) async-start(), calls=%async_computation.2 | async-start | bytes 2228224 | tf_op jit(solution)/shard_map/all_gather | solution.py:137
  728.7 101.5 %all-gather.6.cloned.1.call-start = ((), (), s32[]{:S(2)}) async-start(), calls=%async_computation.3 | async-start | bytes 2228224 | tf_op jit(solution)/shard_map/all_gather | solution.py:138
  729.3 762.0 %reduce-scatter.3.cloned.1.call-start = ((), (), s32[]{:S(2)}) async-start(), calls=%async_computation.4 | async-start | bytes 4227072 | tf_op jit(solution)/shard_map/reduce_scatter | solution.py:184
  729.6 23.0 %copy-start.8 = (s32[8]{0:T(128)S(1)}, s32[8]{0:T(128)}, u32[]{:S(2)}) copy-start(s32[8]{0:T(128)} %param.18) | copy-start | bytes 100
  783.1 49.6 %copy-start.3 = (bf16[4096,128]{1,0:T(8,128)(2,1)S(1)}, bf16[4096,128]{1,0:T(8,128)(2,1)}, u32[]{:S(2)}) copy-start(bf16[4096,128]{1,0:T(8,128)(2,1)} %param.23) | copy-start | bytes 3145732
  842.6 1295.7 %reduce-scatter.5.cloned.1.call-start = ((), (), s32[]{:S(2)}) async-start(), calls=%async_computation.5 | async-start | bytes 4227072 | tf_op jit(solution)/shard_map/reduce_scatter | solution.py:185
Sparse Core Ops, SparseCore 0:
  29.4 35.7 all-gather.7
  130.3 36.0 all-gather.7
  231.5 37.5 all-gather.7
  334.2 37.5 all-gather.7
  422.4 52.1 all-gather.7
  525.1 52.1 all-gather.7
  628.1 51.5 all-gather.7
Sparse Core Ops, SparseCore 1:
  731.0 50.0 all-gather.3
  783.3 46.8 all-gather.5
  842.7 648.6 reduce-scatter.2
  1494.3 644.0 reduce-scatter.4
where the time goes:
time: 2150 us
  waiting for transfers between devices  1960 us (91%)
  matrix products  67.8 us (3%)
  other arithmetic  38.2 us (2%)
  starting transfers between devices  24.6 us (1%)
  blocking collectives  21.7 us (1%)
    reduce_scatter x1, waiting for transfers between devices, on_device(): lax.psum_scatter(up_grad, ('segment', 'fsdp', 'rep'), scatter_dimension=0...  647 us
    reduce_scatter x1, waiting for transfers between devices, on_device(): lax.psum_scatter(down_grad, ('segment', 'fsdp', 'rep'), scatter_dimension...  646 us
    all_gather x7, waiting for transfers between devices, tick_whole(): joined = lax.all_gather(result, 'rep', axis=1, tiled=True)  304 us
    ppermute x7, waiting for transfers between devices, passed_along(): return lax.ppermute(x, axis, pairs)  288 us
    dot_general x4, matrix products, apply_segment(): update = jnp.dot(normed, weight_local, preferred_element_type=jnp.float32)  48.4 us
    all_gather x1, waiting for transfers between devices, on_device(): lax.all_gather(agent_up, 'fsdp', axis=0, tiled=True)  47.1 us
  transfers between devices with their start and end apart: 18, of which 18 were waited for; matrix products, arithmetic and copies ran while one was open for 2% of the time, Pallas kernels for 0%

commit v1 on v0

--- a/solution.py
+++ b/solution.py
@@ -97,7 +97,12 @@
     def tick_whole(tick_pos, state_pair):
         incoming, stored = state_pair
         active, slot_pos, result = segment_step(tick_pos, incoming)
-        joined = lax.all_gather(result, "rep", axis=1, tiled=True)
+        joined = jnp.concatenate(
+            lax.all_to_all(
+                jnp.stack(tuple((result for _ in range(lax.axis_size("rep")))), axis=0), "rep", 0, 0
+            ),
+            axis=1,
+        )
         stored = store_block(stored, active, slot_pos, joined)
         incoming = passed_along(joined, "segment", 1)
         return (incoming, stored)

time: 2150 us -> 1960 us (0.912)
  waiting for transfers between devices: 1960 us -> 1540 us
  blocking collectives: 21.7 us -> 205 us
  starting transfers between devices: 24.6 us -> 75.4 us
    all_gather x7 -> x0, waiting for transfers between devices: 304 us -> none  [tick_whole(): joined = lax.all_gather(result, 'rep', axis=1, tiled=True)]
    all_to_all x0 -> x7, blocking collectives: none -> 165 us  [tick_whole(): lax.all_to_all(jnp.stack(tuple((result for _ in range(lax.axis_size('rep'...]
    ppermute x7, starting transfers between devices: 24.5 us -> 75.2 us  [passed_along(): return lax.ppermute(x, axis, pairs)]
    ppermute x7, waiting for transfers between devices: 288 us -> 238 us  [passed_along(): return lax.ppermute(x, axis, pairs)]
    all_gather x1, waiting for transfers between devices: 47.1 us -> 0.02 us  [on_device(): lax.all_gather(agent_up, 'fsdp', axis=0, tiled=True)]
    all_gather x1, waiting for transfers between devices: 26 us -> 0.02 us  [on_device(): lax.all_gather(agent_down, 'fsdp', axis=0, tiled=True)]
  transfers between devices with their start and end apart: 18 -> 11, of which waited for: 18 -> 9; matrix products, arithmetic and copies ran while one was open for 2% -> 6% of each run, Pallas kernels for 0% -> 0%
where the time goes in v1:
time: 1960 us
  waiting for transfers between devices  1540 us (79%)
  blocking collectives  205 us (10%)
  starting transfers between devices  75.4 us (4%)
  matrix products  68.1 us (3%)
  other arithmetic  40.8 us (2%)
    reduce_scatter x1, waiting for transfers between devices, on_device(): lax.psum_scatter(down_grad, ('segment', 'fsdp', 'rep'), scatter_dimension...  650 us
    reduce_scatter x1, waiting for transfers between devices, on_device(): lax.psum_scatter(up_grad, ('segment', 'fsdp', 'rep'), scatter_dimension=0...  649 us
    ppermute x7, waiting for transfers between devices, passed_along(): return lax.ppermute(x, axis, pairs)  238 us
    all_to_all x7, blocking collectives, tick_whole(): lax.all_to_all(jnp.stack(tuple((result for _ in range(lax.axis_size('rep'...  165 us
    ppermute x7, starting transfers between devices, passed_along(): return lax.ppermute(x, axis, pairs)  75.2 us
    dot_general x4, matrix products, apply_segment(): update = jnp.dot(normed, weight_local, preferred_element_type=jnp.float32)  48.6 us
    psum x1, blocking collectives, spread(): return lax.psum(jnp.where(mine, x, jnp.zeros_like(x)), axis)  40.7 us
  transfers between devices with their start and end apart: 11, of which 9 were waited for; matrix products, arithmetic and copies ran while one was open for 6% of the time, Pallas kernels for 0%

profile of v1, /device:TPU:0, one launch (start us, length us, event | category | flops | bytes accessed | tf_op | source)
XLA Modules:
  0.0 1960.5 jit_solution(17106412016440416015)
XLA Ops:
  8.7 0.8 slice.6
  10.2 0.8 pad_add_fusion
  11.0 1.6 broadcast_in_dim.27
  12.5 4.3 broadcast_in_dim.30
  16.8 576.4 %while.15 = (s32[]{:T(128)}, bf16[256,4096]{1,0:T(8,128)(2,1)}, bf16[1024,4096]{1,0:T(8,128)(2,1)}, s32[]{:T(128)}, s32[1024]{0:T(1024)}, /*index=5*/bf16[128,40...) while((s32[]{:T(128)}, bf16[256,4096]{1,0:T(8,128)(2,1)}, ...), condition=%wide.region_6.7_spmd, body=%wide.region_2.6_spmd.sunk | while | flops 4574970368 | bytes 61890028 | solution.py:114
  16.8 0.8 dynamic_slice.57
  17.6 0.7 convolution_convert_fusion.5
  18.3 15.0 conditional.4
  18.4 2.7 multiply_reduce_fusion
  21.0 12.3 fusion
  33.5 33.6 %all_to_all.10 = bf16[2,256,2048]{2,1,0:T(8,128)(2,1)S(1)} all-to-all(bf16[2,256,2048]{2,1,0:T(8,128)(2,1)S(1)} %pad_maximum_fusion.2), channel_id=1, replica_groups=mesh['segment'=4,'fsdp'=16,'rep'=2] {'rep'}, dimensions={0} | all-to-all | bytes 4194304 | tf_op jit(solution)/shard_map/while/body/eval_jaxpr/all_to_all | solution.py:101
  67.2 2.6 collective-permute-start
  69.9 3.7 select_dynamic-update-slice_fusion.2
  73.6 39.1 %collective-permute-done = bf16[256,4096]{1,0:T(8,128)(2,1)} collective-permute-done((bf16[256,4096]{1,0:T(8,128)(2,1)S(1)}, bf16[256,4096]{1,0:T(8,128)(2,1)}, u32[]{:S(2)}, u32[]{:S(2)}) %collective-permute-start) | collective-permute-done | bytes 2097184 | tf_op jit(solution)/shard_map/while/body/eval_jaxpr/ppermute | solution.py:14
  112.7 0.8 dynamic_slice.57
  114.2 14.8 conditional.4
  114.2 2.7 multiply_reduce_fusion
  116.9 12.1 fusion
  129.2 26.1 %all_to_all.10 = bf16[2,256,2048]{2,1,0:T(8,128)(2,1)S(1)} all-to-all(bf16[2,256,2048]{2,1,0:T(8,128)(2,1)S(1)} %pad_maximum_fusion.2), channel_id=1, replica_groups=mesh['segment'=4,'fsdp'=16,'rep'=2] {'rep'}, dimensions={0} | all-to-all | bytes 4194304 | tf_op jit(solution)/shard_map/while/body/eval_jaxpr/all_to_all | solution.py:101
  155.4 7.4 collective-permute-start
  162.9 3.7 select_dynamic-update-slice_fusion.2
  166.6 37.4 %collective-permute-done = bf16[256,4096]{1,0:T(8,128)(2,1)} collective-permute-done((bf16[256,4096]{1,0:T(8,128)(2,1)S(1)}, bf16[256,4096]{1,0:T(8,128)(2,1)}, u32[]{:S(2)}, u32[]{:S(2)}) %collective-permute-start) | collective-permute-done | bytes 2097184 | tf_op jit(solution)/shard_map/while/body/eval_jaxpr/ppermute | solution.py:14
  204.0 0.8 dynamic_slice.57
  204.7 0.7 convolution_convert_fusion.5
  205.5 14.8 conditional.4
  205.5 2.7 multiply_reduce_fusion
  208.2 12.1 fusion
  220.5 24.4 %all_to_all.10 = bf16[2,256,2048]{2,1,0:T(8,128)(2,1)S(1)} all-to-all(bf16[2,256,2048]{2,1,0:T(8,128)(2,1)S(1)} %pad_maximum_fusion.2), channel_id=1, replica_groups=mesh['segment'=4,'fsdp'=16,'rep'=2] {'rep'}, dimensions={0} | all-to-all | bytes 4194304 | tf_op jit(solution)/shard_map/while/body/eval_jaxpr/all_to_all | solution.py:101
  245.0 7.4 collective-permute-start
  252.4 3.7 select_dynamic-update-slice_fusion.2
  256.2 35.7 %collective-permute-done = bf16[256,4096]{1,0:T(8,128)(2,1)} collective-permute-done((bf16[256,4096]{1,0:T(8,128)(2,1)S(1)}, bf16[256,4096]{1,0:T(8,128)(2,1)}, u32[]{:S(2)}, u32[]{:S(2)}) %collective-permute-start) | collective-permute-done | bytes 2097184 | tf_op jit(solution)/shard_map/while/body/eval_jaxpr/ppermute | solution.py:14
  291.8 0.8 dynamic_slice.57
  293.3 14.8 conditional.4
  293.4 2.7 multiply_reduce_fusion
  296.0 12.1 fusion
  308.3 22.7 %all_to_all.10 = bf16[2,256,2048]{2,1,0:T(8,128)(2,1)S(1)} all-to-all(bf16[2,256,2048]{2,1,0:T(8,128)(2,1)S(1)} %pad_maximum_fusion.2), channel_id=1, replica_groups=mesh['segment'=4,'fsdp'=16,'rep'=2] {'rep'}, dimensions={0} | all-to-all | bytes 4194304 | tf_op jit(solution)/shard_map/while/body/eval_jaxpr/all_to_all | solution.py:101
  331.2 7.4 collective-permute-start
  338.6 3.7 select_dynamic-update-slice_fusion.2
  342.3 33.9 %collective-permute-done = bf16[256,4096]{1,0:T(8,128)(2,1)} collective-permute-done((bf16[256,4096]{1,0:T(8,128)(2,1)S(1)}, bf16[256,4096]{1,0:T(8,128)(2,1)}, u32[]{:S(2)}, u32[]{:S(2)}) %collective-permute-start) | collective-permute-done | bytes 2097184 | tf_op jit(solution)/shard_map/while/body/eval_jaxpr/ppermute | solution.py:14
  376.3 0.8 dynamic_slice.57
  377.0 0.7 convolution_convert_fusion.5
  378.1 21.0 %all_to_all.10 = bf16[2,256,2048]{2,1,0:T(8,128)(2,1)S(1)} all-to-all(bf16[2,256,2048]{2,1,0:T(8,128)(2,1)S(1)} %pad_maximum_fusion.2), channel_id=1, replica_groups=mesh['segment'=4,'fsdp'=16,'rep'=2] {'rep'}, dimensions={0} | all-to-all | bytes 4194304 | tf_op jit(solution)/shard_map/while/body/eval_jaxpr/all_to_all | solution.py:101
  399.2 22.1 %collective-permute-start = (bf16[256,4096]{1,0:T(8,128)(2,1)S(1)}, bf16[256,4096]{1,0:T(8,128)(2,1)}, u32[]{:S(2)}, u32[]{:S(2)}) collective-permute-start(bf16[256,4096]{1,0:T(8,128)(2,1)S(1)} %bitcast.46), channel_id=1, source_target_pairs={{0,32},{32,64},{64,96},{1,33},{33,65},{65,97},{2,34},{34,66},{66,9... | collective-permute-start | bytes 6291464 | tf_op jit(solution)/shard_map/while/body/eval_jaxpr/ppermute | solution.py:14
  421.3 3.7 select_dynamic-update-slice_fusion.2
  425.0 32.2 %collective-permute-done = bf16[256,4096]{1,0:T(8,128)(2,1)} collective-permute-done((bf16[256,4096]{1,0:T(8,128)(2,1)S(1)}, bf16[256,4096]{1,0:T(8,128)(2,1)}, u32[]{:S(2)}, u32[]{:S(2)}) %collective-permute-start) | collective-permute-done | bytes 2097184 | tf_op jit(solution)/shard_map/while/body/eval_jaxpr/ppermute | solution.py:14
  457.3 0.8 dynamic_slice.57
  458.0 0.7 convolution_convert_fusion.5
  459.1 19.2 all_to_all.10
  478.5 5.9 collective-permute-start
  484.4 3.7 select_dynamic-update-slice_fusion.2
  488.1 30.5 %collective-permute-done = bf16[256,4096]{1,0:T(8,128)(2,1)} collective-permute-done((bf16[256,4096]{1,0:T(8,128)(2,1)S(1)}, bf16[256,4096]{1,0:T(8,128)(2,1)}, u32[]{:S(2)}, u32[]{:S(2)}) %collective-permute-start) | collective-permute-done | bytes 2097184 | tf_op jit(solution)/shard_map/while/body/eval_jaxpr/ppermute | solution.py:14
  518.6 0.8 dynamic_slice.57
  519.4 0.7 convolution_convert_fusion.5
  520.5 17.6 all_to_all.10
  538.2 22.3 %collective-permute-start = (bf16[256,4096]{1,0:T(8,128)(2,1)S(1)}, bf16[256,4096]{1,0:T(8,128)(2,1)}, u32[]{:S(2)}, u32[]{:S(2)}) collective-permute-start(bf16[256,4096]{1,0:T(8,128)(2,1)S(1)} %bitcast.46), channel_id=1, source_target_pairs={{0,32},{32,64},{64,96},{1,33},{33,65},{65,97},{2,34},{34,66},{66,9... | collective-permute-start | bytes 6291464 | tf_op jit(solution)/shard_map/while/body/eval_jaxpr/ppermute | solution.py:14
  560.4 3.7 select_dynamic-update-slice_fusion.2
  564.2 29.1 %collective-permute-done = bf16[256,4096]{1,0:T(8,128)(2,1)} collective-permute-done((bf16[256,4096]{1,0:T(8,128)(2,1)S(1)}, bf16[256,4096]{1,0:T(8,128)(2,1)}, u32[]{:S(2)}, u32[]{:S(2)}) %collective-permute-start) | collective-permute-done | bytes 2097184 | tf_op jit(solution)/shard_map/while/body/eval_jaxpr/ppermute | solution.py:14
  593.3 40.7 %psum.7 = f32[8]{0:T(128)S(1)} all-reduce(f32[8]{0:T(128)S(1)} %broadcast_select_fusion), channel_id=1, replica_groups=mesh['segment'=4,'fsdp'=16,'rep'=2] {'segment'}, use_global_device_ids=true, to_apply=%region_14.15 | all-reduce | flops 8 | bytes 64 | tf_op jit(solution)/shard_map/psum | solution.py:19
  638.4 2.1 convolution_convert_fusion.3
  640.5 2.6 multiply_reduce_fusion.2
  647.8 5.2 fusion.13
  653.0 2.7 fusion.29
  655.8 649.6 %reduce-scatter.3.cloned.1.call-done = f32[32,256]{1,0:T(8,128)} async-done(((f32[4096,256]{1,0:T(8,128)}), f32[32,256]{1,0:T(8,128)}) %reduce-scatter.3.cloned.1.call-update) | async-done | bytes 32784 | tf_op jit(solution)/shard_map/reduce_scatter | solution.py:189
  1305.3 648.7 %reduce-scatter.5.cloned.1.call-done = f32[32,256]{1,0:T(8,128)} async-done(((f32[4096,256]{1,0:T(8,128)}), f32[32,256]{1,0:T(8,128)}) %reduce-scatter.5.cloned.1.call-update) | async-done | bytes 32784 | tf_op jit(solution)/shard_map/reduce_scatter | solution.py:190
  (67 shorter events, 12.5 us)
Async XLA Ops:
  7.2 631.2 %all-gather.3.cloned.1.call-start = ((), (), s32[]{:S(2)}) async-start(), calls=%async_computation.3 | async-start | bytes 2228224 | tf_op jit(solution)/shard_map/all_gather | solution.py:142
  7.9 632.6 %all-gather.5.cloned.1.call-start = ((), (), s32[]{:S(2)}) async-start(), calls=%async_computation.4 | async-start | bytes 2228224 | tf_op jit(solution)/shard_map/all_gather | solution.py:143
  8.6 1296.7 %reduce-scatter.3.cloned.1.call-start = ((), (), s32[]{:S(2)}) async-start(), calls=%async_computation.5 | async-start | bytes 4227072 | tf_op jit(solution)/shard_map/reduce_scatter | solution.py:189
  12.5 4.3 copy-start.1
  12.5 4.3 copy-start.4
  16.8 576.4 %copy-start.3 = (f32[4096]{0:T(1024)S(1)}, f32[4096]{0:T(1024)}, u32[]{:S(2)}) copy-start(f32[4096]{0:T(1024)} %param.22) | copy-start | bytes 49156
  67.2 45.5 %collective-permute-start = (bf16[256,4096]{1,0:T(8,128)(2,1)S(1)}, bf16[256,4096]{1,0:T(8,128)(2,1)}, u32[]{:S(2)}, u32[]{:S(2)}) collective-permute-start(bf16[256,4096]{1,0:T(8,128)(2,1)S(1)} %bitcast.46), channel_id=1, source_target_pairs={{0,32},{32,64},{64,96},{1,33},{33,65},{65,97},{2,34},{34,66},{66,9... | collective-permute-start | bytes 6291464 | tf_op jit(solution)/shard_map/while/body/eval_jaxpr/ppermute | solution.py:14
  155.4 48.5 %collective-permute-start = (bf16[256,4096]{1,0:T(8,128)(2,1)S(1)}, bf16[256,4096]{1,0:T(8,128)(2,1)}, u32[]{:S(2)}, u32[]{:S(2)}) collective-permute-start(bf16[256,4096]{1,0:T(8,128)(2,1)S(1)} %bitcast.46), channel_id=1, source_target_pairs={{0,32},{32,64},{64,96},{1,33},{33,65},{65,97},{2,34},{34,66},{66,9... | collective-permute-start | bytes 6291464 | tf_op jit(solution)/shard_map/while/body/eval_jaxpr/ppermute | solution.py:14
  245.0 46.8 %collective-permute-start = (bf16[256,4096]{1,0:T(8,128)(2,1)S(1)}, bf16[256,4096]{1,0:T(8,128)(2,1)}, u32[]{:S(2)}, u32[]{:S(2)}) collective-permute-start(bf16[256,4096]{1,0:T(8,128)(2,1)S(1)} %bitcast.46), channel_id=1, source_target_pairs={{0,32},{32,64},{64,96},{1,33},{33,65},{65,97},{2,34},{34,66},{66,9... | collective-permute-start | bytes 6291464 | tf_op jit(solution)/shard_map/while/body/eval_jaxpr/ppermute | solution.py:14
  331.2 45.1 %collective-permute-start = (bf16[256,4096]{1,0:T(8,128)(2,1)S(1)}, bf16[256,4096]{1,0:T(8,128)(2,1)}, u32[]{:S(2)}, u32[]{:S(2)}) collective-permute-start(bf16[256,4096]{1,0:T(8,128)(2,1)S(1)} %bitcast.46), channel_id=1, source_target_pairs={{0,32},{32,64},{64,96},{1,33},{33,65},{65,97},{2,34},{34,66},{66,9... | collective-permute-start | bytes 6291464 | tf_op jit(solution)/shard_map/while/body/eval_jaxpr/ppermute | solution.py:14
  399.2 58.1 %collective-permute-start = (bf16[256,4096]{1,0:T(8,128)(2,1)S(1)}, bf16[256,4096]{1,0:T(8,128)(2,1)}, u32[]{:S(2)}, u32[]{:S(2)}) collective-permute-start(bf16[256,4096]{1,0:T(8,128)(2,1)S(1)} %bitcast.46), channel_id=1, source_target_pairs={{0,32},{32,64},{64,96},{1,33},{33,65},{65,97},{2,34},{34,66},{66,9... | collective-permute-start | bytes 6291464 | tf_op jit(solution)/shard_map/while/body/eval_jaxpr/ppermute | solution.py:14
  478.5 40.1 %collective-permute-start = (bf16[256,4096]{1,0:T(8,128)(2,1)S(1)}, bf16[256,4096]{1,0:T(8,128)(2,1)}, u32[]{:S(2)}, u32[]{:S(2)}) collective-permute-start(bf16[256,4096]{1,0:T(8,128)(2,1)S(1)} %bitcast.46), channel_id=1, source_target_pairs={{0,32},{32,64},{64,96},{1,33},{33,65},{65,97},{2,34},{34,66},{66,9... | collective-permute-start | bytes 6291464 | tf_op jit(solution)/shard_map/while/body/eval_jaxpr/ppermute | solution.py:14
  538.2 55.1 %collective-permute-start = (bf16[256,4096]{1,0:T(8,128)(2,1)S(1)}, bf16[256,4096]{1,0:T(8,128)(2,1)}, u32[]{:S(2)}, u32[]{:S(2)}) collective-permute-start(bf16[256,4096]{1,0:T(8,128)(2,1)S(1)} %bitcast.46), channel_id=1, source_target_pairs={{0,32},{32,64},{64,96},{1,33},{33,65},{65,97},{2,34},{34,66},{66,9... | collective-permute-start | bytes 6291464 | tf_op jit(solution)/shard_map/while/body/eval_jaxpr/ppermute | solution.py:14
  593.3 42.0 %copy-start.5 = (s32[8]{0:T(128)S(1)}, s32[8]{0:T(128)}, u32[]{:S(2)}) copy-start(s32[8]{0:T(128)} %param.18) | copy-start | bytes 100
  640.5 2.6 copy-start.2
  653.0 1301.0 %reduce-scatter.5.cloned.1.call-start = ((), (), s32[]{:S(2)}) async-start(), calls=%async_computation.6 | async-start | bytes 4227072 | tf_op jit(solution)/shard_map/reduce_scatter | solution.py:190
Sparse Core Ops, SparseCore 0:
  10.4 57.4 all-gather.2
  70.3 44.3 all-gather.4
  653.1 652.1 reduce-scatter.2
  1308.1 645.8 reduce-scatter.4
